TPU v7x, 256 devices: a whole 4x4x8 slice. The times are simulated.
256 devices in a mesh: tm: 4 (over y), row: 4 (over x), col: 16 (over z, core).
Axes of the slice: x: 4, y: 4, z: 8, core: 2. Of those that a mesh axis runs over, the one named last changes fastest.
Arguments:
- day_block: float32 [4, 4, 16, 32, 4, 4, 128], P('tm', None, 'col', None, None, 'row'), as said below
- left_coupling: float32 [4, 4, 16, 32, 4, 4, 128], P('tm', None, 'col', None, None, 'row'), may hold values from -0.125 to 0.125
- right_coupling: float32 [4, 4, 16, 32, 4, 4, 128], P('tm', None, 'col', None, None, 'row'), may hold values from -0.125 to 0.125
- separator_block: float32 [4, 4, 16, 32, 4, 4, 128], P('tm', None, 'col', None, None, 'row')
- arrow_coupling: float32 [4, 4, 16, 32, 64], P('tm', None, 'col'), may hold values from -0.125 to 0.125
- arrow_block: float32 [64, 64], replicated
Outputs:
- day_factor: float32 [4, 4, 16, 32, 4, 4, 128], P('tm', None, 'col', None, None, 'row')
- left_factor: float32 [4, 4, 16, 32, 4, 4, 128], P('tm', None, 'col', None, None, 'row')
- right_factor: float32 [4, 4, 16, 32, 4, 4, 128], P('tm', None, 'col', None, None, 'row')
- arrow_factor: float32 [4, 4, 16, 32, 64], P('tm', None, 'col')
- separator: float32 [4, 4, 16, 32, 4, 4, 128], P('tm', None, 'col', None, None, 'row')
- arrowhead: float32 [64, 64], replicated
Inputs may be any that keep to these rules, and one draw needn't show every extreme that they name: Each group's day_block and separator_block, and arrow_block, is an exactly symmetric matrix with all eigenvalues at least 1.
All inputs are finite; a program needn't handle non-finite values.
Results may differ from a plain program's by a relative error of at most 0.0001.
Values sent between devices are 32-bit elements; how exact they have to be, the bound alone decides.
No kernel may reach another device: no remote copies, remote signals or barrier semaphores. Data moves between devices by JAX's collectives and lax.ppermute only.
A program may use at most 128 MiB of HBM per device.

v0:
```python
import jax
import jax.numpy as jnp
from jax import lax
from jax.sharding import PartitionSpec as P


def passed_along(value, axis, steps):
    count = lax.axis_size(axis)
    initial, last = (max(0, -steps), min(count, count - steps))
    return lax.ppermute(value, axis, [(source, source + steps) for source in range(initial, last)])


def product(left, right):
    return jnp.dot(left, right, precision=lax.Precision.HIGHEST, preferred_element_type=jnp.float32)


def lower_inverse(factor):
    identity = jnp.eye(factor.shape[0], dtype=jnp.float32)
    return lax.linalg.triangular_solve(factor, identity, left_side=True, lower=True)


def reorder_nodes(whole, panels, col_width):
    count = whole.shape[0]
    col_count = lax.axis_size("col")
    spread = whole.reshape(count, panels, col_count, col_width)
    return jnp.transpose(spread, (2, 1, 3, 0)).reshape(col_count * panels * col_width, count)


def separator_term(solved, panels, col_width, row_width):
    whole = lax.all_gather(
        solved.reshape(solved.shape[0], panels, 1, row_width), "row", axis=2, tiled=True
    )
    ordered = reorder_nodes(whole, panels, col_width)
    return lax.psum_scatter(product(ordered, solved), "col", scatter_dimension=0, tiled=True)


def product_tn(left, right):
    return lax.dot_general(
        left,
        right,
        (((0,), (0,)), ((), ())),
        precision=lax.Precision.HIGHEST,
        preferred_element_type=jnp.float32,
    )


def per_device(
    day_block, left_coupling, right_coupling, separator_block, arrow_coupling, arrow_block
):
    panels = day_block.shape[1]
    col_width = day_block.shape[3]
    row_width = day_block.shape[6]
    col_count = lax.axis_size("col")
    row_count = lax.axis_size("row")
    panel_size = col_width * col_count
    arrow_rows = arrow_block.shape[0]
    col_index = lax.axis_index("col")
    row_index = lax.axis_index("row")
    matrix = day_block.reshape(panels, col_width, panels, row_width)
    left_part = left_coupling.reshape(panels, col_width, panels * row_width)
    right_part = right_coupling.reshape(panels, col_width, panels * row_width)
    arrow_part = arrow_coupling.reshape(panels, col_width, arrow_rows)

    def gather_block_row(k, after):
        piece = matrix[k, :, k:, :]
        if after is not None:
            piece, _ = lax.optimization_barrier((piece, after))
        by_col = lax.all_gather(piece, "col", axis=0, tiled=True)
        whole = lax.all_gather(by_col[:, :, None, :], "row", axis=2, tiled=True)
        return whole.reshape(panel_size, (panels - k) * panel_size)

    def gather_coupling(k, after):
        pieces = (left_part[k], right_part[k])
        if after is not None:
            pieces, _ = lax.optimization_barrier((pieces, after))
        return tuple((lax.all_gather(piece, "col", axis=0, tiled=True) for piece in pieces))

    block_rows = [gather_block_row(0, None)] + [None] * (panels - 1)
    left_full = [None] * panels
    right_full = [None] * panels
    left_full[0], right_full[0] = gather_coupling(0, None)
    arrow_all = lax.all_gather(arrow_part, "col", axis=1, tiled=True)
    arrow_full = [arrow_all[k] for k in range(panels)]
    pending = [[] for _ in range(panels)]
    pending_left = [[] for _ in range(panels)]
    pending_right = [[] for _ in range(panels)]
    rows_at = col_index * col_width + lax.broadcasted_iota(jnp.int32, (col_width, row_width), 0)
    cols_at = row_index * row_width + lax.broadcasted_iota(jnp.int32, (col_width, row_width), 1)
    per_slice = row_width // col_width
    owner = col_index // per_slice
    offset = col_index % per_slice * col_width

    def own_columns(solved):
        spread = solved.reshape(panel_size, panels, row_width)
        picked = lax.dynamic_slice_in_dim(spread, offset, col_width, 2)
        picked = jnp.where(row_index == owner, picked, 0.0)
        return lax.psum(picked, "row").reshape(panel_size, panels * col_width)

    factor_blocks = []
    left_solved = []
    right_solved = []
    arrow_solved = []
    right_term = jnp.zeros((panels * col_width, panels * row_width), jnp.float32)
    left_term = jnp.zeros((panels * col_width, panels * row_width), jnp.float32)
    arrow_term = jnp.zeros((arrow_rows, arrow_rows), jnp.float32)
    for current in range(panels):
        remain = panels - current
        block_row = block_rows[current]
        for update in pending[current]:
            block_row = block_row - update
        diagonal_full = block_row[:, :panel_size]
        factor = jnp.linalg.cholesky(diagonal_full)
        if remain > 1:
            block_rows[current + 1] = gather_block_row(current + 1, factor)
            fresh_left, fresh_right = gather_coupling(current + 1, factor)
            for update in pending_left[current + 1]:
                fresh_left = fresh_left - update
            for update in pending_right[current + 1]:
                fresh_right = fresh_right - update
            left_full[current + 1], right_full[current + 1] = (fresh_left, fresh_right)
        inverse = lower_inverse(factor)
        owned_full = product(inverse, block_row)
        owned = lax.dynamic_slice_in_dim(
            owned_full.reshape(panel_size, remain, row_count, row_width), row_index, 1, 2
        ).reshape(panel_size, remain, row_width)
        solved_left = product(inverse, left_full[current])
        solved_right = product(inverse, right_full[current])
        solved_arrow = product(inverse, arrow_full[current])
        left_solved.append(solved_left)
        right_solved.append(solved_right)
        arrow_solved.append(solved_arrow)
        right_term = right_term + product_tn(own_columns(solved_right), solved_right)
        left_term = left_term + product_tn(own_columns(solved_left), solved_left)
        arrow_term = arrow_term + product_tn(solved_arrow, solved_arrow)
        mine_rows = lax.dynamic_slice_in_dim(owned, col_index * col_width, col_width, 0)
        diagonal_part = jnp.where(cols_at >= rows_at, mine_rows[:, 0, :], 0.0)
        factor_blocks.append(
            jnp.concatenate(
                [
                    jnp.zeros((col_width, current, row_width), jnp.float32),
                    diagonal_part[:, None, :],
                    mine_rows[:, 1:, :],
                ],
                axis=1,
            )
        )
        if remain > 1:
            later = owned_full[:, panel_size:]
            for step in range(remain - 1):
                target = current + 1 + step
                rows = slice(step * panel_size, (step + 1) * panel_size)
                pending[target].append(product_tn(later[:, rows], later[:, step * panel_size :]))
            left_update = product_tn(later, solved_left)
            right_update = product_tn(later, solved_right)
            arrow_update = product_tn(later, solved_arrow)
            for step in range(remain - 1):
                rows = slice(step * panel_size, (step + 1) * panel_size)
                target = current + 1 + step
                if step == 0:
                    left_full[target] = left_full[target] - left_update[rows]
                    right_full[target] = right_full[target] - right_update[rows]
                else:
                    pending_left[target].append(left_update[rows])
                    pending_right[target].append(right_update[rows])
                arrow_full[target] = arrow_full[target] - arrow_update[rows]
    day_factor = jnp.stack(factor_blocks).reshape(day_block.shape)

    def mine(parts, width):
        whole = jnp.stack(parts).reshape(panels, col_count, col_width, width)
        return lax.dynamic_index_in_dim(whole, col_index, 1, keepdims=False)

    left_out = mine(left_solved, panels * row_width)
    right_out = mine(right_solved, panels * row_width)
    arrow_out = mine(arrow_solved, arrow_rows)
    separator_local = separator_block.reshape(panels * col_width, panels * row_width)
    from_next = passed_along(left_term, "tm", -1)
    separator = separator_local - right_term - from_next
    arrow_total = jnp.sum(lax.all_gather(arrow_term, "tm", axis=0, tiled=False), axis=0)
    arrowhead = arrow_block - arrow_total
    return (
        day_factor,
        left_out.reshape(left_coupling.shape),
        right_out.reshape(right_coupling.shape),
        arrow_out.reshape(arrow_coupling.shape),
        separator.reshape(separator_block.shape),
        arrowhead,
    )


def solution(mesh):
    return jax.shard_map(
        per_device,
        mesh=mesh,
        in_specs=(
            P("tm", None, "col", None, None, "row", None),
            P("tm", None, "col", None, None, "row", None),
            P("tm", None, "col", None, None, "row", None),
            P("tm", None, "col", None, None, "row", None),
            P("tm", None, "col", None, None),
            P(),
        ),
        out_specs=(
            P("tm", None, "col", None, None, "row", None),
            P("tm", None, "col", None, None, "row", None),
            P("tm", None, "col", None, None, "row", None),
            P("tm", None, "col", None, None),
            P("tm", None, "col", None, None, "row", None),
            P(),
        ),
        check_vma=False,
    )
```

profile of v0, /device:TPU:8, one launch (start us, length us, event | category | flops | bytes accessed | tf_op | source)
XLA Modules:
  0.0 1049.3 jit_solution(13707844531146109400)
XLA Ops:
  8.9 43.0 %all-gather.37.cloned.1.call-done = f32[1,1,1,512,4,1,128]{6,4,5,2,1,0,3:T(4,128)} async-done(((f32[1,1,1,32,4,1,128]{6,4,5,2,1,0,3:T(4,128)}), f32[1,1,1,512,4,1,128]{6,4,5,2,1,0,3:T(4,128)}) %all-gather.37.cloned.1.call-update) | async-done | bytes 1048592 | tf_op jit(solution)/shard_map/all_gather | solution.py:68
  57.8 18.4 %all-gather.5 = f32[1,4,1,512,64]{4,1,2,0,3:T(4,128)S(1)} all-gather(f32[1,4,1,32,64]{4,1,2,0,3:T(4,128)S(1)} %copy.85), channel_id=7, replica_groups=mesh['tm'=4,'row'=4,'col'=16] {'col'}, dimensions={3}, use_global_device_ids=true | all-gather | bytes 557056 | tf_op jit(solution)/shard_map/all_gather | solution.py:82
  76.9 26.8 %all-gather.39.cloned.1.call-done = f32[1,1,1,512,4,4,128]{6,3,4,2,1,0,5:T(8,128)} async-done(((f32[1,1,1,512,4,1,128]{6,3,4,2,1,0,5:T(8,128)}), f32[1,1,1,512,4,4,128]{6,3,4,2,1,0,5:T(8,128)}) %all-gather.39.cloned.1.call-update) | async-done | bytes 4194320 | tf_op jit(solution)/shard_map/all_gather | solution.py:69
  112.2 11.7 %cholesky.462 = f32[128,128]{1,0:T(8,128)S(1)} custom-call(f32[128,128]{1,0:T(8,128)S(1)} %cholesky.746), custom_call_target="Cholesky" | custom-call | tf_op jit(solution)/shard_map/jit(cholesky)/cholesky | solution.py:112
  135.2 12.5 %cholesky.481 = f32[128,128]{1,0:T(8,128)S(1)} custom-call(f32[128,128]{1,0:T(8,128)} %cholesky.750), custom_call_target="Cholesky" | custom-call | tf_op jit(solution)/shard_map/jit(cholesky)/cholesky | solution.py:112
  160.3 11.7 %cholesky.502 = f32[128,128]{1,0:T(8,128)S(1)} custom-call(f32[128,128]{1,0:T(8,128)S(1)} %cholesky.755), custom_call_target="Cholesky" | custom-call | tf_op jit(solution)/shard_map/jit(cholesky)/cholesky | solution.py:112
  182.4 11.7 %cholesky.519 = f32[128,128]{1,0:T(8,128)S(1)} custom-call(f32[128,128]{1,0:T(8,128)S(1)} %convolution_subtract_fusion.30), custom_call_target="Cholesky" | custom-call | tf_op jit(solution)/shard_map/jit(cholesky)/cholesky | solution.py:112
  199.0 21.4 %all_gather.59 = f32[512,3,128]{2,0,1:T(8,128)} all-gather(f32[32,3,128]{2,0,1:T(8,128)} %slice_bitcast_fusion.32), channel_id=1, replica_groups=mesh['tm'=4,'row'=4,'col'=16] {'col'}, dimensions={0}, use_global_device_ids=true | all-gather | bytes 835584 | tf_op jit(solution)/shard_map/all_gather | solution.py:68
  238.9 39.3 %custom-call.38 = f32[4,128,128]{1,2,0:T(8,128)S(1)} custom-call(f32[4,128,128]{2,1,0:T(8,128)S(1)} %get-tuple-element.52), custom_call_target="InvertDiagBlocksLowerTriangular" | custom-call | tf_op jit(solution)/shard_map/triangular_solve/custom-call.3 | solution.py:19
  356.2 11.7 %cholesky.534 = f32[128,128]{1,0:T(8,128)S(1)} custom-call(f32[128,128]{1,0:T(8,128)S(1)} %cholesky.759), custom_call_target="Cholesky" | custom-call | tf_op jit(solution)/shard_map/jit(cholesky)/cholesky | solution.py:112
  380.4 11.7 %cholesky.553 = f32[128,128]{1,0:T(8,128)S(1)} custom-call(f32[128,128]{1,0:T(8,128)S(1)} %cholesky.763), custom_call_target="Cholesky" | custom-call | tf_op jit(solution)/shard_map/jit(cholesky)/cholesky | solution.py:112
  403.9 11.7 %cholesky.574 = f32[128,128]{1,0:T(8,128)S(1)} custom-call(f32[128,128]{1,0:T(8,128)S(1)} %cholesky.768), custom_call_target="Cholesky" | custom-call | tf_op jit(solution)/shard_map/jit(cholesky)/cholesky | solution.py:112
  427.0 11.7 %cholesky.591 = f32[128,128]{1,0:T(8,128)S(1)} custom-call(f32[128,128]{1,0:T(8,128)S(1)} %convolution_subtract_fusion.29), custom_call_target="Cholesky" | custom-call | tf_op jit(solution)/shard_map/jit(cholesky)/cholesky | solution.py:112
  444.2 17.9 %all_gather.61 = f32[512,2,128]{2,1,0:T(2,128)} all-gather(f32[32,2,128]{2,1,0:T(2,128)S(1)} %copy.73), channel_id=1, replica_groups=mesh['tm'=4,'row'=4,'col'=16] {'col'}, dimensions={0}, use_global_device_ids=true | all-gather | bytes 557056 | tf_op jit(solution)/shard_map/all_gather | solution.py:68
  470.2 39.3 %custom-call.42 = f32[4,128,128]{1,2,0:T(8,128)S(1)} custom-call(f32[4,128,128]{2,1,0:T(8,128)S(1)} %get-tuple-element.53), custom_call_target="InvertDiagBlocksLowerTriangular" | custom-call | tf_op jit(solution)/shard_map/triangular_solve/custom-call.3 | solution.py:19
  572.8 11.7 %cholesky.606 = f32[128,128]{1,0:T(8,128)S(1)} custom-call(f32[128,128]{1,0:T(8,128)S(1)} %cholesky.772), custom_call_target="Cholesky" | custom-call | tf_op jit(solution)/shard_map/jit(cholesky)/cholesky | solution.py:112
  598.7 11.7 %cholesky.625 = f32[128,128]{1,0:T(8,128)S(1)} custom-call(f32[128,128]{1,0:T(8,128)S(1)} %cholesky.776), custom_call_target="Cholesky" | custom-call | tf_op jit(solution)/shard_map/jit(cholesky)/cholesky | solution.py:112
  624.9 11.7 %cholesky.646 = f32[128,128]{1,0:T(8,128)S(1)} custom-call(f32[128,128]{1,0:T(8,128)S(1)} %cholesky.781), custom_call_target="Cholesky" | custom-call | tf_op jit(solution)/shard_map/jit(cholesky)/cholesky | solution.py:112
  649.3 11.7 %cholesky.663 = f32[128,128]{1,0:T(8,128)S(1)} custom-call(f32[128,128]{1,0:T(8,128)S(1)} %convolution_subtract_fusion.28), custom_call_target="Cholesky" | custom-call | tf_op jit(solution)/shard_map/jit(cholesky)/cholesky | solution.py:112
  679.7 39.9 %custom-call.46 = f32[4,128,128]{1,2,0:T(8,128)} custom-call(f32[4,128,128]{2,1,0:T(8,128)S(1)} %get-tuple-element.54), custom_call_target="InvertDiagBlocksLowerTriangular" | custom-call | tf_op jit(solution)/shard_map/triangular_solve/custom-call.3 | solution.py:19
  719.6 17.3 %all_gather.63 = f32[512,1,128]{2,0,1:T(8,128)} all-gather(f32[32,1,128]{2,0,1:T(8,128)S(1)} %copy-done.73), channel_id=1, replica_groups=mesh['tm'=4,'row'=4,'col'=16] {'col'}, dimensions={0}, use_global_device_ids=true | all-gather | bytes 278528 | tf_op jit(solution)/shard_map/all_gather | solution.py:68
  894.6 40.3 %custom-call.50 = f32[4,128,128]{1,2,0:T(8,128)} custom-call(f32[4,128,128]{2,1,0:T(8,128)S(1)} %get-tuple-element.55), custom_call_target="InvertDiagBlocksLowerTriangular" | custom-call | tf_op jit(solution)/shard_map/triangular_solve/custom-call.3 | solution.py:19
  973.7 12.0 %all-gather.6 = f32[256,64]{1,0:T(8,128)S(1)} all-gather(f32[64,64]{1,0:T(8,128)S(1)} %convolution_add_fusion.6), channel_id=8, replica_groups=mesh['tm'=4,'row'=4,'col'=16] {'tm'}, dimensions={0}, use_global_device_ids=true | all-gather | bytes 81920 | tf_op jit(solution)/shard_map/all_gather | solution.py:178
  992.5 32.9 %all-reduce.5.cloned.1.call-done = (f32[512,128]{0,1:T(8,128)}, f32[512,128]{0,1:T(8,128)}, f32[512,128]{0,1:T(8,128)}, f32[512,128]{0,1:T(8,128)}, f32[512,128]...) async-done(((f32[512,128]{0,1:T(8,128)}, f32[512,128]{0,1:T(8,128)}, f32[512,128]{0,1:T(8,128)}, f32[512,128]{0,1:T(8,128)}, ...) | async-done | bytes 2097168 | tf_op jit(solution)/shard_map/psum | solution.py:97
  (501 shorter events, 571.8 us)
Async XLA Ops:
  7.2 50.6 %copy-start.50 = (f32[1,4,1,32,4,1,128]{6,5,4,3,2,1,0:T(1,128)S(1)}, f32[1,4,1,32,4,1,128]{6,5,4,3,2,1,0:T(1,128)}, u32[]{:S(2)}) copy-start(f32[1,4,1,32,4,1,128]{6,5,4,3,2,1,0:T(1,128)} %param.9) | copy-start | bytes 786436
  7.2 47.1 %copy-start.66 = (f32[1,4,1,32,4,1,128]{6,5,4,3,2,1,0:T(1,128)S(1)}, f32[1,4,1,32,4,1,128]{6,5,4,3,2,1,0:T(1,128)}, u32[]{:S(2)}) copy-start(f32[1,4,1,32,4,1,128]{6,5,4,3,2,1,0:T(1,128)} %param.10) | copy-start | bytes 786436
  7.2 50.6 %copy-start.74 = (f32[1,4,1,32,64]{4,3,2,1,0:T(8,128)S(1)}, f32[1,4,1,32,64]{4,3,2,1,0:T(8,128)}, u32[]{:S(2)}) copy-start(f32[1,4,1,32,64]{4,3,2,1,0:T(8,128)} %param.13) | copy-start | bytes 98308
  7.2 44.7 %all-gather.37.cloned.1.call-start = ((), (), s32[]{:S(2)}) async-start(), calls=%async_computation.8 | async-start | bytes 1114112 | tf_op jit(solution)/shard_map/all_gather | solution.py:68
  8.8 94.8 %all-gather.39.cloned.1.call-start = ((), (), s32[]{:S(2)}) async-start(), calls=%async_computation.9 | async-start | bytes 5242880 | tf_op jit(solution)/shard_map/all_gather | solution.py:69
  54.2 245.2 %all-gather.29.cloned.1.call-start = ((), (), s32[]{:S(2)}) async-start(), calls=%async_computation.4 | async-start | bytes 1114112 | tf_op jit(solution)/shard_map/all_gather | solution.py:76
  57.0 245.6 %all-gather.21.cloned.1.call-start = ((), (), s32[]{:S(2)}) async-start(), calls=%async_computation | async-start | bytes 1114112 | tf_op jit(solution)/shard_map/all_gather | solution.py:76
  57.7 280.7 %all-gather.41.cloned.1.call-start = ((), (), s32[]{:S(2)}) async-start(), calls=%async_computation.10 | async-start | bytes 3932160 | tf_op jit(solution)/shard_map/all_gather | solution.py:69
  220.4 294.3 %all-gather.31.cloned.1.call-start = ((), (), s32[]{:S(2)}) async-start(), calls=%async_computation.5 | async-start | bytes 1114112 | tf_op jit(solution)/shard_map/all_gather | solution.py:76
  228.1 54.7 %copy-start.8 = (f32[512,512]{1,0:T(8,128)}, f32[512,512]{1,0:T(8,128)S(1)}, u32[]{:S(2)}) copy-start(f32[512,512]{1,0:T(8,128)S(1)} %fusion.39) | copy-start | bytes 3145732
  299.2 220.4 %all-gather.23.cloned.1.call-start = ((), (), s32[]{:S(2)}) async-start(), calls=%async_computation.1 | async-start | bytes 1114112 | tf_op jit(solution)/shard_map/all_gather | solution.py:76
  338.3 217.1 %all-gather.43.cloned.1.call-start = ((), (), s32[]{:S(2)}) async-start(), calls=%async_computation.11 | async-start | bytes 2621440 | tf_op jit(solution)/shard_map/all_gather | solution.py:69
  368.1 76.1 %copy-start.71 = (f32[32,2,128]{2,0,1:T(8,128)S(1)}, f32[32,2,128]{2,0,1:T(8,128)}, u32[]{:S(2)}) copy-start(f32[32,2,128]{2,0,1:T(8,128)} %slice_bitcast_fusion.33) | copy-start | bytes 98308
  402.3 107.2 %copy-start.9 = (f32[512,512]{1,0:T(8,128)S(1)}, f32[512,512]{1,0:T(8,128)}, u32[]{:S(2)}) copy-start(f32[512,512]{1,0:T(8,128)} %copy-done.8) | copy-start | bytes 3145732
  462.1 284.1 %all-gather.33.cloned.1.call-start = ((), (), s32[]{:S(2)}) async-start(), calls=%async_computation.6 | async-start | bytes 1114112 | tf_op jit(solution)/shard_map/all_gather | solution.py:76
  527.5 226.3 %all-gather.25.cloned.1.call-start = ((), (), s32[]{:S(2)}) async-start(), calls=%async_computation.2 | async-start | bytes 1114112 | tf_op jit(solution)/shard_map/all_gather | solution.py:76
  555.3 228.9 %all-gather.45.cloned.1.call-start = ((), (), s32[]{:S(2)}) async-start(), calls=%async_computation.12 | async-start | bytes 1310720 | tf_op jit(solution)/shard_map/all_gather | solution.py:69
  597.4 122.2 %copy-start.73 = (f32[32,1,128]{2,0,1:T(8,128)S(1)}, f32[32,1,128]{2,0,1:T(8,128)}, u32[]{:S(2)}) copy-start(f32[32,1,128]{2,0,1:T(8,128)} %slice_bitcast_fusion.34) | copy-start | bytes 49156
  737.0 206.5 %all-gather.35.cloned.1.call-start = ((), (), s32[]{:S(2)}) async-start(), calls=%async_computation.7 | async-start | bytes 1114112 | tf_op jit(solution)/shard_map/all_gather | solution.py:76
  746.1 208.8 %all-gather.27.cloned.1.call-start = ((), (), s32[]{:S(2)}) async-start(), calls=%async_computation.3 | async-start | bytes 1114112 | tf_op jit(solution)/shard_map/all_gather | solution.py:76
  783.8 241.7 %all-reduce.5.cloned.1.call-start = ((), (), s32[]{:S(2)}) async-start(), calls=%async_computation.13 | async-start | bytes 4194304 | tf_op jit(solution)/shard_map/psum | solution.py:97
  817.3 117.7 %copy-start.10 = (f32[512,512]{1,0:T(8,128)S(1)}, f32[512,512]{1,0:T(8,128)}, u32[]{:S(2)}) copy-start(f32[512,512]{1,0:T(8,128)} %copy-done.8) | copy-start | bytes 3145732
  894.6 48.9 %copy-start.2 = (f32[512,1024]{1,0:T(8,128)S(1)}, f32[512,1024]{1,0:T(8,128)}, u32[]{:S(2)}) copy-start(f32[512,1024]{1,0:T(8,128)} %fusion.178) | copy-start | bytes 6291460
  1031.3 9.8 collective-permute-start
  (66 other events, 665.9 us)
Sparse Core Ops, SparseCore 0:
  10.4 41.4 all-gather.36
  54.3 49.2 all-gather.38
  105.5 38.9 all-gather.28
  146.2 37.4 all-gather.20
  220.5 42.9 all-gather.40
  299.3 36.2 all-gather.30
  338.4 36.4 all-gather.22
  462.2 35.6 all-gather.42
  527.6 36.7 all-gather.32
  566.1 37.2 all-gather.24
  737.1 24.4 all-gather.44
  763.3 38.9 all-gather.34
  804.1 37.3 all-gather.26
  963.8 61.6 all-reduce.4
where the time goes:
time: 1060 us; the launch traced here: 1050 us
  other arithmetic  509 us (48%)
  matrix products  188 us (18%)
  local copies, waits for them, and re-layouts  126 us (12%)
  waiting for transfers between devices  109 us (10%)
  blocking collectives  87 us (8%)
  between operations  26.4 us (2%)
    another operation x59, other arithmetic, per_device(): factor = jnp.linalg.cholesky(diagonal_full)  321 us
    another operation x9, other arithmetic, lower_inverse(): lax.linalg.triangular_solve(factor, identity, left_side=True, lower=True)  163 us
    dot_general x27, matrix products, product_tn(): lax.dot_general(left, right, (((0,), (0,)), ((), ())), precision=lax.Prec...  79.9 us
    dot_general x16, matrix products, product(): jnp.dot(left, right, precision=lax.Precision.HIGHEST, preferred_element_t...  60.9 us
    all_gather x3, blocking collectives, gather_block_row(): by_col = lax.all_gather(piece, 'col', axis=0, tiled=True)  56.5 us
    all_gather x1, waiting for transfers between devices, gather_block_row(): by_col = lax.all_gather(piece, 'col', axis=0, tiled=True)  43 us
    another operation x53, local copies, waits for them, and re-layouts, lower_inverse(): lax.linalg.triangular_solve(factor, identity, left_side=True, lower=True)  38.9 us
    psum x1, waiting for transfers between devices, own_columns(): return lax.psum(picked, 'row').reshape(panel_size, panels * col_width)  32.9 us
  transfers between devices with their start and end apart: 15, of which 4 were waited for; matrix products, arithmetic and copies ran while one was open for 76% of the time, Pallas kernels for 0%

commit v1 on v0

--- a/solution.py
+++ b/solution.py
@@ -2,6 +2,7 @@
 import jax.numpy as jnp
 from jax import lax
 from jax.sharding import PartitionSpec as P
+from jax.lax import all_gather
 
 
 def passed_along(value, axis, steps):
@@ -94,7 +95,9 @@
         spread = solved.reshape(panel_size, panels, row_width)
         picked = lax.dynamic_slice_in_dim(spread, offset, col_width, 2)
         picked = jnp.where(row_index == owner, picked, 0.0)
-        return lax.psum(picked, "row").reshape(panel_size, panels * col_width)
+        return jnp.sum(all_gather(picked, axis_name="row"), 0).reshape(
+            panel_size, panels * col_width
+        )
 
     factor_blocks = []
     left_solved = []

time: 1060 us -> 1140 us (1.075)
  local copies, waits for them, and re-layouts: 126 us -> 176 us
  other arithmetic: 509 us -> 542 us
  waiting for transfers between devices: 109 us -> 88.7 us
  matrix products: 188 us -> 201 us
    all_gather x0 -> x8, local copies, waits for them, and re-layouts: none -> 37.1 us  [own_columns(): all_gather(picked, axis_name='row')]
    psum x1 -> x0, waiting for transfers between devices: 32.9 us -> none  [own_columns(): return lax.psum(picked, 'row').reshape(panel_size, panels * col_width)]
    reduce_sum x0 -> x8, other arithmetic: none -> 30.9 us  [own_columns(): jnp.sum(all_gather(picked, axis_name='row'), 0)]
    all_gather x4, waiting for transfers between devices: 26.8 us -> 45.2 us  [gather_block_row(): whole = lax.all_gather(by_col[:, :, None, :], 'row', axis=2, tiled=True)]
    dot_general x27, matrix products: 79.9 us -> 92.9 us  [product_tn(): lax.dot_general(left, right, (((0,), (0,)), ((), ())), precision=lax.Prec...]
  transfers between devices with their start and end apart: 15 -> 22, of which waited for: 4 -> 2; matrix products, arithmetic and copies ran while one was open for 76% -> 80% of each run, Pallas kernels for 0% -> 0%
where the time goes in v1:
time: 1140 us; the launch traced here: 1130 us
  other arithmetic  542 us (48%)
  matrix products  201 us (18%)
  local copies, waits for them, and re-layouts  176 us (15%)
  waiting for transfers between devices  88.7 us (8%)
  blocking collectives  88.3 us (8%)
  between operations  27 us (2%)
    another operation x59, other arithmetic, per_device(): factor = jnp.linalg.cholesky(diagonal_full)  327 us
    another operation x9, other arithmetic, lower_inverse(): lax.linalg.triangular_solve(factor, identity, left_side=True, lower=True)  161 us
    dot_general x27, matrix products, product_tn(): lax.dot_general(left, right, (((0,), (0,)), ((), ())), precision=lax.Prec...  92.9 us
    dot_general x16, matrix products, product(): jnp.dot(left, right, precision=lax.Precision.HIGHEST, preferred_element_t...  62.1 us
    all_gather x3, blocking collectives, gather_block_row(): by_col = lax.all_gather(piece, 'col', axis=0, tiled=True)  56.3 us
    all_gather x4, waiting for transfers between devices, gather_block_row(): whole = lax.all_gather(by_col[:, :, None, :], 'row', axis=2, tiled=True)  45.2 us
    all_gather x1, waiting for transfers between devices, gather_block_row(): by_col = lax.all_gather(piece, 'col', axis=0, tiled=True)  43 us
    all_gather x8, local copies, waits for them, and re-layouts, own_columns(): all_gather(picked, axis_name='row')  37.1 us
  transfers between devices with their start and end apart: 22, of which 2 were waited for; matrix products, arithmetic and copies ran while one was open for 80% of the time, Pallas kernels for 0%

profile of v1, /device:TPU:8, one launch (start us, length us, event | category | flops | bytes accessed | tf_op | source)
XLA Modules:
  0.0 1128.6 jit_solution(1553343991441988533)
XLA Ops:
  8.8 43.0 %all-gather.53.cloned.1.call-done = f32[1,1,1,512,4,1,128]{6,4,5,2,1,0,3:T(4,128)} async-done(((f32[1,1,1,32,4,1,128]{6,4,5,2,1,0,3:T(4,128)}), f32[1,1,1,512,4,1,128]{6,4,5,2,1,0,3:T(4,128)}) %all-gather.53.cloned.1.call-update) | async-done | bytes 1048592 | tf_op jit(solution)/shard_map/all_gather | solution.py:69
  58.4 45.2 %all-gather.55.cloned.1.call-done = f32[1,1,1,512,4,4,128]{6,3,4,2,1,0,5:T(8,128)} async-done(((f32[1,1,1,512,4,1,128]{6,3,4,2,1,0,5:T(8,128)}), f32[1,1,1,512,4,4,128]{6,3,4,2,1,0,5:T(8,128)}) %all-gather.55.cloned.1.call-update) | async-done | bytes 4194320 | tf_op jit(solution)/shard_map/all_gather | solution.py:70
  112.1 11.7 %cholesky.462 = f32[128,128]{1,0:T(8,128)S(1)} custom-call(f32[128,128]{1,0:T(8,128)S(1)} %cholesky.746), custom_call_target="Cholesky" | custom-call | tf_op jit(solution)/shard_map/jit(cholesky)/cholesky | solution.py:115
  134.5 11.7 %cholesky.481 = f32[128,128]{1,0:T(8,128)S(1)} custom-call(f32[128,128]{1,0:T(8,128)S(1)} %cholesky.750), custom_call_target="Cholesky" | custom-call | tf_op jit(solution)/shard_map/jit(cholesky)/cholesky | solution.py:115
  157.1 11.7 %cholesky.502 = f32[128,128]{1,0:T(8,128)S(1)} custom-call(f32[128,128]{1,0:T(8,128)S(1)} %cholesky.755), custom_call_target="Cholesky" | custom-call | tf_op jit(solution)/shard_map/jit(cholesky)/cholesky | solution.py:115
  179.3 11.7 %cholesky.519 = f32[128,128]{1,0:T(8,128)S(1)} custom-call(f32[128,128]{1,0:T(8,128)S(1)} %convolution_subtract_fusion.30), custom_call_target="Cholesky" | custom-call | tf_op jit(solution)/shard_map/jit(cholesky)/cholesky | solution.py:115
  195.9 21.0 %all_gather.107 = f32[512,3,128]{2,0,1:T(8,128)} all-gather(f32[32,3,128]{2,0,1:T(8,128)S(1)} %slice_bitcast_fusion.32), channel_id=1, replica_groups=mesh['tm'=4,'row'=4,'col'=16] {'col'}, dimensions={0}, use_global_device_ids=true | all-gather | bytes 835584 | tf_op jit(solution)/shard_map/all_gather | solution.py:69
  226.6 39.3 %custom-call.38 = f32[4,128,128]{1,2,0:T(8,128)S(1)} custom-call(f32[4,128,128]{2,1,0:T(8,128)S(1)} %get-tuple-element.52), custom_call_target="InvertDiagBlocksLowerTriangular" | custom-call | tf_op jit(solution)/shard_map/triangular_solve/custom-call.3 | solution.py:20
  319.0 12.5 %cholesky.534 = f32[128,128]{1,0:T(8,128)S(1)} custom-call(f32[128,128]{1,0:T(8,128)} %cholesky.759), custom_call_target="Cholesky" | custom-call | tf_op jit(solution)/shard_map/jit(cholesky)/cholesky | solution.py:115
  344.1 11.7 %cholesky.553 = f32[128,128]{1,0:T(8,128)S(1)} custom-call(f32[128,128]{1,0:T(8,128)S(1)} %cholesky.763), custom_call_target="Cholesky" | custom-call | tf_op jit(solution)/shard_map/jit(cholesky)/cholesky | solution.py:115
  367.4 11.7 %cholesky.574 = f32[128,128]{1,0:T(8,128)S(1)} custom-call(f32[128,128]{1,0:T(8,128)S(1)} %cholesky.768), custom_call_target="Cholesky" | custom-call | tf_op jit(solution)/shard_map/jit(cholesky)/cholesky | solution.py:115
  390.4 11.7 %cholesky.591 = f32[128,128]{1,0:T(8,128)S(1)} custom-call(f32[128,128]{1,0:T(8,128)S(1)} %convolution_subtract_fusion.29), custom_call_target="Cholesky" | custom-call | tf_op jit(solution)/shard_map/jit(cholesky)/cholesky | solution.py:115
  408.4 17.8 %all_gather.109 = f32[512,2,128]{2,1,0:T(2,128)} all-gather(f32[32,2,128]{2,1,0:T(2,128)S(1)} %copy.65), channel_id=1, replica_groups=mesh['tm'=4,'row'=4,'col'=16] {'col'}, dimensions={0}, use_global_device_ids=true | all-gather | bytes 557056 | tf_op jit(solution)/shard_map/all_gather | solution.py:69
  435.4 39.3 %custom-call.42 = f32[4,128,128]{1,2,0:T(8,128)S(1)} custom-call(f32[4,128,128]{2,1,0:T(8,128)S(1)} %get-tuple-element.53), custom_call_target="InvertDiagBlocksLowerTriangular" | custom-call | tf_op jit(solution)/shard_map/triangular_solve/custom-call.3 | solution.py:20
  505.2 18.2 %all-gather.5 = f32[1,4,1,512,64]{4,1,2,0,3:T(4,128)S(1)} all-gather(f32[1,4,1,32,64]{4,1,2,0,3:T(4,128)S(1)} %copy.77), channel_id=7, replica_groups=mesh['tm'=4,'row'=4,'col'=16] {'col'}, dimensions={3}, use_global_device_ids=true | all-gather | bytes 557056 | tf_op jit(solution)/shard_map/all_gather | solution.py:83
  594.6 11.7 %cholesky.606 = f32[128,128]{1,0:T(8,128)S(1)} custom-call(f32[128,128]{1,0:T(8,128)S(1)} %cholesky.772), custom_call_target="Cholesky" | custom-call | tf_op jit(solution)/shard_map/jit(cholesky)/cholesky | solution.py:115
  648.8 13.2 %cholesky.646 = f32[128,128]{1,0:T(8,128)} custom-call(f32[128,128]{1,0:T(8,128)} %cholesky.781), custom_call_target="Cholesky" | custom-call | tf_op jit(solution)/shard_map/jit(cholesky)/cholesky | solution.py:115
  678.4 11.7 %cholesky.663 = f32[128,128]{1,0:T(8,128)S(1)} custom-call(f32[128,128]{1,0:T(8,128)S(1)} %convolution_subtract_fusion.28), custom_call_target="Cholesky" | custom-call | tf_op jit(solution)/shard_map/jit(cholesky)/cholesky | solution.py:115
  700.5 17.5 %all_gather.111 = f32[512,1,128]{2,0,1:T(8,128)} all-gather(f32[32,1,128]{2,0,1:T(8,128)} %slice_bitcast_fusion.34), channel_id=1, replica_groups=mesh['tm'=4,'row'=4,'col'=16] {'col'}, dimensions={0}, use_global_device_ids=true | all-gather | bytes 278528 | tf_op jit(solution)/shard_map/all_gather | solution.py:69
  780.5 39.9 %custom-call.46 = f32[4,128,128]{1,2,0:T(8,128)} custom-call(f32[4,128,128]{2,1,0:T(8,128)S(1)} %get-tuple-element.54), custom_call_target="InvertDiagBlocksLowerTriangular" | custom-call | tf_op jit(solution)/shard_map/triangular_solve/custom-call.3 | solution.py:20
  878.8 11.7 %cholesky.678 = f32[128,128]{1,0:T(8,128)S(1)} custom-call(f32[128,128]{1,0:T(8,128)S(1)} %cholesky.785), custom_call_target="Cholesky" | custom-call | tf_op jit(solution)/shard_map/jit(cholesky)/cholesky | solution.py:115
  902.6 11.7 %cholesky.697 = f32[128,128]{1,0:T(8,128)S(1)} custom-call(f32[128,128]{1,0:T(8,128)S(1)} %cholesky.789), custom_call_target="Cholesky" | custom-call | tf_op jit(solution)/shard_map/jit(cholesky)/cholesky | solution.py:115
  973.9 39.3 %custom-call.50 = f32[4,128,128]{1,2,0:T(8,128)S(1)} custom-call(f32[4,128,128]{2,1,0:T(8,128)S(1)} %get-tuple-element.55), custom_call_target="InvertDiagBlocksLowerTriangular" | custom-call | tf_op jit(solution)/shard_map/triangular_solve/custom-call.3 | solution.py:20
  1089.1 13.8 %all-gather.14 = f32[256,64]{1,0:T(8,128)S(1)} all-gather(f32[64,64]{1,0:T(8,128)} %convolution_add_fusion.6), channel_id=16, replica_groups=mesh['tm'=4,'row'=4,'col'=16] {'tm'}, dimensions={0}, use_global_device_ids=true | all-gather | bytes 81920 | tf_op jit(solution)/shard_map/all_gather | solution.py:181
  (540 shorter events, 648.0 us)
Async XLA Ops:
  7.2 44.7 %all-gather.53.cloned.1.call-start = ((), (), s32[]{:S(2)}) async-start(), calls=%async_computation.8 | async-start | bytes 1114112 | tf_op jit(solution)/shard_map/all_gather | solution.py:69
  8.8 94.8 %all-gather.55.cloned.1.call-start = ((), (), s32[]{:S(2)}) async-start(), calls=%async_computation.9 | async-start | bytes 5242880 | tf_op jit(solution)/shard_map/all_gather | solution.py:70
  54.2 215.9 %all-gather.37.cloned.1.call-start = ((), (), s32[]{:S(2)}) async-start(), calls=%async_computation | async-start | bytes 1114112 | tf_op jit(solution)/shard_map/all_gather | solution.py:77
  56.9 218.9 %all-gather.45.cloned.1.call-start = ((), (), s32[]{:S(2)}) async-start(), calls=%async_computation.4 | async-start | bytes 1114112 | tf_op jit(solution)/shard_map/all_gather | solution.py:77
  57.6 242.5 %all-gather.57.cloned.1.call-start = ((), (), s32[]{:S(2)}) async-start(), calls=%async_computation.10 | async-start | bytes 3932160 | tf_op jit(solution)/shard_map/all_gather | solution.py:70
  216.9 264.0 %all-gather.39.cloned.1.call-start = ((), (), s32[]{:S(2)}) async-start(), calls=%async_computation.1 | async-start | bytes 1114112 | tf_op jit(solution)/shard_map/all_gather | solution.py:77
  218.2 277.2 %all-gather.47.cloned.1.call-start = ((), (), s32[]{:S(2)}) async-start(), calls=%async_computation.5 | async-start | bytes 1114112 | tf_op jit(solution)/shard_map/all_gather | solution.py:77
  266.0 284.6 %all-gather.71.cloned.1.call-start = ((), (), s32[]{:S(2)}) async-start(), calls=%async_computation.17 | async-start | bytes 1310720 | tf_op jit(solution)/shard_map/all_gather | solution.py:98
  274.3 284.6 %all-gather.63.cloned.1.call-start = ((), (), s32[]{:S(2)}) async-start(), calls=%async_computation.13 | async-start | bytes 1310720 | tf_op jit(solution)/shard_map/all_gather | solution.py:98
  300.0 277.2 %all-gather.59.cloned.1.call-start = ((), (), s32[]{:S(2)}) async-start(), calls=%async_computation.11 | async-start | bytes 2621440 | tf_op jit(solution)/shard_map/all_gather | solution.py:70
  365.8 108.9 %copy-start.11 = (f32[512,512]{1,0:T(8,128)S(1)}, f32[512,512]{1,0:T(8,128)}, u32[]{:S(2)}) copy-start(f32[512,512]{1,0:T(8,128)} %copy-done.10) | copy-start | bytes 3145732
  426.3 315.1 %all-gather.73.cloned.1.call-start = ((), (), s32[]{:S(2)}) async-start(), calls=%async_computation.18 | async-start | bytes 1310720 | tf_op jit(solution)/shard_map/all_gather | solution.py:98
  487.5 264.6 %all-gather.65.cloned.1.call-start = ((), (), s32[]{:S(2)}) async-start(), calls=%async_computation.14 | async-start | bytes 1310720 | tf_op jit(solution)/shard_map/all_gather | solution.py:98
  500.1 329.5 %all-gather.41.cloned.1.call-start = ((), (), s32[]{:S(2)}) async-start(), calls=%async_computation.2 | async-start | bytes 1114112 | tf_op jit(solution)/shard_map/all_gather | solution.py:77
  527.9 326.2 %all-gather.49.cloned.1.call-start = ((), (), s32[]{:S(2)}) async-start(), calls=%async_computation.6 | async-start | bytes 1114112 | tf_op jit(solution)/shard_map/all_gather | solution.py:77
  577.2 290.7 %all-gather.61.cloned.1.call-start = ((), (), s32[]{:S(2)}) async-start(), calls=%async_computation.12 | async-start | bytes 1310720 | tf_op jit(solution)/shard_map/all_gather | solution.py:70
  718.0 304.7 %all-gather.43.cloned.1.call-start = ((), (), s32[]{:S(2)}) async-start(), calls=%async_computation.3 | async-start | bytes 1114112 | tf_op jit(solution)/shard_map/all_gather | solution.py:77
  739.7 297.7 %all-gather.51.cloned.1.call-start = ((), (), s32[]{:S(2)}) async-start(), calls=%async_computation.7 | async-start | bytes 1114112 | tf_op jit(solution)/shard_map/all_gather | solution.py:77
  820.5 227.7 %all-gather.75.cloned.1.call-start = ((), (), s32[]{:S(2)}) async-start(), calls=%async_computation.19 | async-start | bytes 1310720 | tf_op jit(solution)/shard_map/all_gather | solution.py:98
  838.9 218.5 %all-gather.67.cloned.1.call-start = ((), (), s32[]{:S(2)}) async-start(), calls=%async_computation.15 | async-start | bytes 1310720 | tf_op jit(solution)/shard_map/all_gather | solution.py:98
  867.7 205.0 %all-gather.77.cloned.1.call-start = ((), (), s32[]{:S(2)}) async-start(), calls=%async_computation.20 | async-start | bytes 1310720 | tf_op jit(solution)/shard_map/all_gather | solution.py:98
  901.2 112.1 %copy-start.12 = (f32[512,512]{1,0:T(8,128)S(1)}, f32[512,512]{1,0:T(8,128)}, u32[]{:S(2)}) copy-start(f32[512,512]{1,0:T(8,128)} %copy-done.10) | copy-start | bytes 3145732
  1035.1 75.3 %all-gather.69.cloned.1.call-start = ((), (), s32[]{:S(2)}) async-start(), calls=%async_computation.16 | async-start | bytes 1310720 | tf_op jit(solution)/shard_map/all_gather | solution.py:98
  1086.5 32.3 %collective-permute-start = (f32[128,512]{1,0:T(8,128)}, f32[128,512]{1,0:T(8,128)}, u32[]{:S(2)}, u32[]{:S(2)}) collective-permute-start(f32[128,512]{1,0:T(8,128)} %convolution_add_fusion), channel_id=1, source_target_pairs={{64,0},{128,64},{192,128},{65,1},{129,65},{193,129},{66,2},{130,66... | collective-permute-start | bytes 786440 | tf_op jit(solution)/shard_map/ppermute | solution.py:11
  (70 other events, 773.2 us)
Sparse Core Ops, SparseCore 0:
  10.4 41.4 all-gather.52
  54.3 49.2 all-gather.54
  106.0 39.0 all-gather.36
  147.3 37.6 all-gather.44
  217.0 43.3 all-gather.56
  262.1 38.8 all-gather.38
  302.8 37.2 all-gather.46
  341.9 25.3 all-gather.70
  369.1 27.4 all-gather.62
  426.4 35.5 all-gather.58
  487.6 24.8 all-gather.72
  514.2 27.0 all-gather.64
  543.0 38.9 all-gather.40
  583.7 37.3 all-gather.48
  718.1 24.7 all-gather.60
  744.6 39.0 all-gather.42
  820.6 36.7 all-gather.50
  859.1 25.1 all-gather.74
  886.1 27.2 all-gather.66
  1035.2 24.8 all-gather.76
  1062.0 26.9 all-gather.68
